TPU v7x, 256 devices: a whole 4x4x8 slice. The times are simulated.
256 devices in a mesh: lat: 8 (over z), lev: 32 (over x, y, core).
Axes of the slice: x: 4, y: 4, z: 8, core: 2. Of those that a mesh axis runs over, the one named last changes fastest.
Arguments:
- spec_in: bfloat16 [32, 640, 1281], P('lev', 'lat'), may hold values from -6 to 6
- legendre: bfloat16 [640, 1280, 1281], P('lat', 'lev'), may hold values from -0.15625 to 0.15625
- gauss_weights: float32 [1280], P('lev'), may hold values from 0.1 to 1
- row_points: int32 [2, 1280], P(None, 'lev'), may hold values from 4 to 5120
Outputs:
- spec_out: bfloat16 [32, 640, 1281], P('lev', 'lat')
All inputs are finite; a program needn't handle non-finite values.
Results may differ from a plain program's by a relative error of at most 0.02.
Values may be sent and summed in bfloat16 or wider, within the bound.
No kernel may reach another device: no remote copies, remote signals or barrier semaphores. Data moves between devices by JAX's collectives and lax.ppermute only.
A program may use at most 128 MiB of HBM per device.

v0:
```python
import math
import jax
import jax.numpy as jnp
from jax import lax
from jax.sharding import PartitionSpec as P

NLON = 5120
SLOT_CODES = (0, 0, 1, 1)
PARITY_CODES = (0, 1, 0, 1)


def pair_masks(first_pair, pair_count, packed):
    pair_ids = first_pair + jnp.arange(pair_count, dtype=jnp.int32)
    positions = jnp.arange(packed, dtype=jnp.int32)
    boundary = packed - 1 - pair_ids
    in_second = (positions[None, :] >= boundary[:, None]).astype(jnp.int32)
    degree = positions[None, :] - in_second * boundary[:, None]
    parity = degree % 2
    slot_codes = jnp.array(SLOT_CODES, dtype=jnp.int32)
    parity_codes = jnp.array(PARITY_CODES, dtype=jnp.int32)
    return (in_second[:, :, None] == slot_codes) & (parity[:, :, None] == parity_codes)


def wave_tables(total_pairs, truncation):
    pair_ids = jnp.arange(total_pairs, dtype=jnp.int32)
    wavenumbers = jnp.stack([pair_ids, truncation - pair_ids], axis=1)
    longitudes = jnp.arange(NLON, dtype=jnp.int32)
    phases = wavenumbers[:, :, None] * longitudes[None, None, :] % NLON
    angles = phases.astype(jnp.float32) * (2.0 * math.pi / NLON)
    return (jnp.cos(angles).astype(jnp.bfloat16), jnp.sin(angles).astype(jnp.bfloat16), wavenumbers)


def fourier_work(spectrum, row_counts, cosines, sines, wavenumbers, truncation):
    kept_mask = (2 * wavenumbers[:, None, :] < row_counts[None, :, None]).astype(jnp.float32)
    masked = spectrum * kept_mask[..., None].astype(jnp.bfloat16)
    half_channels = spectrum.shape[-1] // 2
    levels = half_channels // 2
    real_part = masked[..., :half_channels]
    imag_part = masked[..., half_channels:]
    grid_values = jnp.einsum(
        "plsf,psk->lfk", real_part, cosines, preferred_element_type=jnp.float32
    )
    grid_values = (
        grid_values
        - jnp.einsum("plsf,psk->lfk", imag_part, sines, preferred_element_type=jnp.float32)
    ) * (1.0 / math.sqrt(truncation + 1))
    vortex = grid_values[:, :levels]
    divergence = grid_values[:, levels:]
    products = jnp.concatenate(
        [vortex * divergence, 0.5 * (vortex * vortex - divergence * divergence)], axis=1
    ).astype(jnp.bfloat16)
    scale_back = 4.0 / math.sqrt(NLON)
    real_out = (
        jnp.einsum("lfk,psk->plsf", products, cosines, preferred_element_type=jnp.float32)
        * scale_back
    )
    imag_out = (
        -jnp.einsum("lfk,psk->plsf", products, sines, preferred_element_type=jnp.float32)
        * scale_back
    )
    return (jnp.concatenate([real_out, imag_out], axis=-1) * kept_mask[..., None]).astype(
        jnp.bfloat16
    )


def local(spec_in, legendre, gauss_weights, row_points):
    pair_count, lat_count, packed = legendre.shape
    truncation = packed - 2
    groups = lax.axis_size("lat")
    local_channels = spec_in.shape[0]
    channels = local_channels * lax.axis_size("lev")
    tile_size = math.gcd(pair_count, 8)
    tile_count = pair_count // tile_size
    first_pair = lax.axis_index("lat") * pair_count
    selector = pair_masks(first_pair, pair_count, packed)
    select_half = selector.astype(jnp.bfloat16).reshape(tile_count, tile_size, packed, 4)
    select_full = selector.astype(jnp.float32).reshape(tile_count, tile_size, packed, 4)
    legendre_tiles = legendre.reshape(tile_count, tile_size, lat_count, packed)
    gathered = lax.all_gather(spec_in, "lev", axis=0, tiled=True)
    piece_width = gathered.shape[0]
    spectral = jnp.moveaxis(gathered.reshape(piece_width, tile_count, tile_size, packed), 1, 0)

    def inverse_tile(inputs):
        legendre_tile, spectral_tile, select_tile = inputs
        spread = spectral_tile[None] * jnp.moveaxis(select_tile, 2, 0)[:, None]
        return jnp.einsum(
            "pjq,xcpq->pjxc", legendre_tile, spread, preferred_element_type=jnp.float32
        )

    tile_sums = lax.map(inverse_tile, (legendre_tiles, spectral, select_half))
    legendre_sums = tile_sums.reshape(pair_count, lat_count, 4, piece_width)
    even_part = legendre_sums[:, :, 0::2]
    odd_part = legendre_sums[:, :, 1::2]
    fourier = jnp.concatenate([even_part + odd_part, even_part - odd_part], axis=1).astype(
        jnp.bfloat16
    )
    cosines, sines, wavenumbers = wave_tables(pair_count * groups, truncation)
    local_rows = row_points.reshape(1, 2 * lat_count)
    band_lats = 2 * lat_count // groups
    lat_rows = lax.all_to_all(fourier, "lat", split_axis=1, concat_axis=0, tiled=True)
    my_rows = lax.dynamic_slice_in_dim(local_rows[0], lax.axis_index("lat") * band_lats, band_lats)
    answered = fourier_work(lat_rows, my_rows, cosines, sines, wavenumbers, truncation)
    answered = answered.reshape(groups, pair_count, band_lats, 2, channels)
    returned = lax.all_to_all(answered, "lat", split_axis=0, concat_axis=0, tiled=True)
    back = jnp.moveaxis(returned, 0, 1).reshape(pair_count, 2 * lat_count, 2, channels)
    north_rows = back[:, :lat_count].astype(jnp.float32)
    south_rows = back[:, lat_count:].astype(jnp.float32)
    weights = gauss_weights[None, :, None, None]
    weighted = jnp.stack(
        [weights * (north_rows + south_rows), weights * (north_rows - south_rows)], axis=3
    )
    weighted = weighted.reshape(pair_count, lat_count, 4, channels).astype(jnp.bfloat16)
    part_tiles = weighted.reshape(
        tile_count, tile_size, lat_count, 4, local_channels * lax.axis_size("lev")
    )

    def direct_tile(inputs):
        legendre_tile, weighted_tile, select_tile = inputs
        full_sums = jnp.einsum(
            "pjq,pjxc->pqxc", legendre_tile, weighted_tile, preferred_element_type=jnp.float32
        )
        picked = jnp.sum(full_sums * select_tile[:, :, :, None], axis=2)
        return jnp.moveaxis(picked, 2, 0)

    picked_tiles = lax.map(direct_tile, (legendre_tiles, part_tiles, select_full))
    return lax.psum_scatter(
        jnp.moveaxis(picked_tiles, 0, 1)
        .reshape(local_channels * lax.axis_size("lev"), pair_count, packed)
        .astype(jnp.bfloat16),
        "lev",
        scatter_dimension=0,
        tiled=True,
    )


def solution(mesh):
    return jax.shard_map(
        local,
        mesh=mesh,
        in_specs=(P("lev", "lat", None), P("lat", "lev", None), P("lev"), P(None, "lev")),
        out_specs=P("lev", "lat", None),
        check_vma=False,
    )
```

profile of v0, /device:TPU:2, one launch (start us, length us, event | category | flops | bytes accessed | tf_op | source)
XLA Modules:
  0.0 796.2 jit_solution(10550959991378505809)
XLA Ops:
  7.7 2.7 fusion.74
  10.4 57.7 %all-gather.2.cloned.1.call-done = bf16[32,80,1281]{2,1,0:T(8,128)(2,1)} async-done(((bf16[1,80,1281]{2,1,0:T(8,128)(2,1)}), bf16[32,80,1281]{2,1,0:T(8,128)(2,1)}) %all-gather.2.cloned.1.call-update) | async-done | bytes 6558736 | tf_op jit(solution)/shard_map/all_gather | solution.py:79
  68.2 7.5 copy.45
  75.6 45.0 %while.20 = (s32[]{:T(128)}, f32[10,8,40,4,32]{2,4,3,1,0:T(8,128)}, bf16[10,8,40,1281]{3,2,1,0:T(8,128)(2,1)}, bf16[10,32,8,1281]{3,1,2,0:T(8,128)(2,1)}, bf16[10,8,1281,4]{2,3,1,0:T(4,128)(2,1)S(1)}, /*index=5*/s32[]{:T(128)}) while((s32[]{:T(128)}, f32[10,8,40,4,32]{2,4,3,1,0:T(8,128)}, bf16[10,8,40,1281]{3,2,1,0:T(8,128)(2,1)}, ...), condition=%wide.region_1.2_spmd, body=%wide.region_0.1_spmd.sunk | while | flops 106251264 | bytes 9575181 | solution.py:90
  77.2 2.1 fusion.110
  86.2 2.1 fusion.110
  90.7 2.1 fusion.110
  108.7 2.1 fusion.110
  113.2 2.1 fusion.110
  120.6 3.4 add_convert_fusion
  124.7 3.5 copy.32
  128.2 7.0 all-to-all-start
  135.6 34.4 %all-to-all-done = bf16[80,80,2,32]{0,3,2,1:T(8,128)(2,1)S(1)} async-done(((bf16[80,80,2,32]{0,3,2,1:T(8,128)(2,1)}), bf16[80,80,2,32]{0,3,2,1:T(8,128)(2,1)S(1)}, u32[]{:S(2)}, u32[]{:S(2)}) %all-to-all-start) | async-done | bytes 819232 | tf_op jit(solution)/shard_map/all_to_all | solution.py:100
  172.2 103.9 %fusion.27 = f32[10,16,5120]{2,1,0:T(8,128)S(1)} fusion(s32[640,2]{0,1:T(2,128)S(1)} %get-tuple-element.90, bf16[640,10,2,16]{0,3,2,1:T(8,128)(2,1)S(1)} %fusion.96), kind=kOutput, calls=%fused_computation.38 | convolution fusion | flops 2162688000 | bytes 3691520 | tf_op jit(solution)/shard_map/plsf,psk->lfk/dot_general | solution.py:45
  276.1 103.4 %fusion.30 = f32[10,16,5120]{2,1,0:T(8,128)S(1)} fusion(f32[10,16,5120]{2,1,0:T(8,128)S(1)} %fusion.27, s32[640,2]{0,1:T(2,128)S(1)} %get-tuple-element.90, bf16[640,10,2,16]{0,3,2,1:T(8,128)(2,1)S(1)} %fusion.98), kind=kOutput, calls=%fused_computation.39 | convolution fusion | flops 2164326400 | bytes 6968320 | tf_op jit(solution)/shard_map/plsf,psk->lfk/dot_general | solution.py:40
  381.3 103.4 %fusion.41 = f32[640,10,2,16]{0,3,1,2:T(8,128)S(1)} fusion(s32[640,2]{0,1:T(2,128)S(1)} %get-tuple-element.90, bf16[10,16,5120,1]{2,1,0,3:T(8,128)(2,1)S(1)} %maximum_bitcast_fusion.9), kind=kOutput, calls=%fused_computation.57 | convolution fusion | flops 2162892800 | bytes 2462720 | tf_op jit(solution)/shard_map/lfk,psk->plsf/dot_general | solution.py:54
  485.5 107.6 %fusion.50 = f32[640,10,2,16]{0,3,1,2:T(8,128)S(1)} fusion(s32[640,2]{0,1:T(2,128)S(1)} %get-tuple-element.90, bf16[10,16,5120,1]{2,1,0,3:T(8,128)(2,1)} %maximum_bitcast_fusion.10), kind=kOutput, calls=%fused_computation.60 | convolution fusion | flops 2163097600 | bytes 2462720 | tf_op jit(solution)/shard_map/lfk,psk->plsf/dot_general | solution.py:58
  595.6 3.6 all-to-all-start.1
  599.2 34.7 %all-to-all-done.1 = bf16[8,80,10,2,32]{1,4,3,2,0:T(8,128)(2,1)S(1)} async-done(((bf16[8,80,10,2,32]{1,4,3,2,0:T(8,128)(2,1)}), bf16[8,80,10,2,32]{1,4,3,2,0:T(8,128)(2,1)S(1)}, u32[]{:S(2)}, u32[]{:S(2)}) %all-to-all-start.1) | async-done | bytes 819232 | tf_op jit(solution)/shard_map/all_to_all | solution.py:104
  635.7 5.9 copy.36
  641.6 46.5 %while.21 = (s32[]{:T(128)}, bf16[10,32,8,1281]{3,1,2,0:T(8,128)(2,1)}, bf16[10,8,40,1281]{3,2,1,0:T(8,128)(2,1)}, bf16[10,8,40,4,32]{2,4,3,1,0:T(8,128)(2,1)S(1)}, f32[10,8,1281,4]{2,3,1,0:T(4,128)}, /*index=5*/s32[]{:T(128)}) while((s32[]{:T(128)}, bf16[10,32,8,1281]{3,1,2,0:T(8,128)(2,1)}, bf16[10,8,40,1281]{3,2,1,0:T(8,128)(2,1)}, ...), condition=%wide.region_4.5_spmd, body=%wide.region_2.4_spmd.sunk | while | flops 107235072 | bytes 14686669 | solution.py:125
  660.3 2.1 fusion.113
  688.1 8.4 %copy.44 = bf16[32,10,8,1281]{3,2,1,0:T(8,128)(2,1)} copy(bf16[32,10,8,1281]{3,0,2,1:T(8,128)(2,1)} %bitcast.110) | data formatting | bytes 13117440 | tf_op jit(solution)/shard_map/convert_element_type | solution.py:129
  696.6 92.5 %reduce-scatter.2.cloned.1.call-done = bf16[1,80,1281]{2,1,0:T(8,128)(2,1)} async-done(((bf16[32,80,1281]{2,1,0:T(8,128)(2,1)}), bf16[1,80,1281]{2,1,0:T(8,128)(2,1)}) %reduce-scatter.2.cloned.1.call-update) | async-done | bytes 204976 | tf_op jit(solution)/shard_map/reduce_scatter | solution.py:126
  (132 shorter events, 89.9 us)
Async XLA Ops:
  6.5 61.6 %all-gather.2.cloned.1.call-start = ((), (), s32[]{:S(2)}) async-start(), calls=%async_computation.3 | async-start | bytes 7434240 | tf_op jit(solution)/shard_map/all_gather | solution.py:79
  124.7 10.5 %copy-start.1 = (s32[2,40]{1,0:T(2,128)S(1)}, s32[2,40]{1,0:T(2,128)}, u32[]{:S(2)}) copy-start(s32[2,40]{1,0:T(2,128)} %param.13) | copy-start | bytes 964
  128.2 41.8 %all-to-all-start = ((bf16[80,80,2,32]{0,3,2,1:T(8,128)(2,1)}), bf16[80,80,2,32]{0,3,2,1:T(8,128)(2,1)S(1)}, u32[]{:S(2)}, u32[]{:S(2)}) async-start(bf16[80,80,2,32]{0,3,2,1:T(8,128)(2,1)} %copy.32), calls=%async_computation | async-start | bytes 2621440 | tf_op jit(solution)/shard_map/all_to_all | solution.py:100
  594.0 39.9 %copy-start = (f32[40]{0:T(128)S(1)}, f32[40]{0:T(128)}, u32[]{:S(2)}) copy-start(f32[40]{0:T(128)} %param.12) | copy-start | bytes 484
  595.6 38.3 %all-to-all-start.1 = ((bf16[8,80,10,2,32]{1,4,3,2,0:T(8,128)(2,1)}), bf16[8,80,10,2,32]{1,4,3,2,0:T(8,128)(2,1)S(1)}, u32[]{:S(2)}, u32[]{:S(2)}) async-start(bf16[8,80,10,2,32]{1,4,3,2,0:T(8,128)(2,1)} %fusion.33), calls=%async_computation.1 | async-start | bytes 2621440 | tf_op jit(solution)/shard_map/all_to_all | solution.py:104
  599.2 190.0 %reduce-scatter.2.cloned.1.call-start = ((), (), s32[]{:S(2)}) async-start(), calls=%async_computation.4 | async-start | bytes 7434240 | tf_op jit(solution)/shard_map/reduce_scatter | solution.py:126
Sparse Core Ops, SparseCore 0:
  10.0 58.1 all-gather.1
  696.7 92.3 reduce-scatter.1
where the time goes:
time: 804 us; the launch traced here: 796 us
  matrix products  460 us (57%)
  waiting for transfers between devices  220 us (27%)
  local copies, waits for them, and re-layouts  68.9 us (9%)
  other arithmetic  22.8 us (3%)
  between operations  13.9 us (2%)
  starting transfers between devices  10.6 us (1%)
    dot_general x1, matrix products, fourier_work(): jnp.einsum('lfk,psk->plsf', products, sines, preferred_element_type=jnp.f...  108 us
    dot_general x1, matrix products, fourier_work(): jnp.einsum('plsf,psk->lfk', imag_part, sines, preferred_element_type=jnp....  104 us
    dot_general x1, matrix products, fourier_work(): jnp.einsum('plsf,psk->lfk', real_part, cosines, preferred_element_type=jn...  103 us
    dot_general x1, matrix products, fourier_work(): jnp.einsum('lfk,psk->plsf', products, cosines, preferred_element_type=jnp...  103 us
    reduce_scatter x1, waiting for transfers between devices, local(): lax.psum_scatter(jnp.moveaxis(picked_tiles, 0, 1).reshape(local_channels...  92.5 us
    all_gather x1, waiting for transfers between devices, local(): gathered = lax.all_gather(spec_in, 'lev', axis=0, tiled=True)  57.7 us
    while x20, matrix products  41.2 us
    all_to_all x1, waiting for transfers between devices, local(): lax.all_to_all(answered, 'lat', split_axis=0, concat_axis=0, tiled=True)  34.7 us
  transfers between devices with their start and end apart: 4, of which 4 were waited for; matrix products, arithmetic and copies ran while one was open for 0% of the time, Pallas kernels for 0%

commit v1 on v0

--- a/solution.py
+++ b/solution.py
@@ -97,7 +97,10 @@
     cosines, sines, wavenumbers = wave_tables(pair_count * groups, truncation)
     local_rows = row_points.reshape(1, 2 * lat_count)
     band_lats = 2 * lat_count // groups
-    lat_rows = lax.all_to_all(fourier, "lat", split_axis=1, concat_axis=0, tiled=True)
+    lat_rows = jnp.concatenate(
+        lax.all_to_all(jnp.stack(jnp.split(fourier, lax.axis_size("lat"), axis=1)), "lat", 0, 0),
+        axis=0,
+    )
     my_rows = lax.dynamic_slice_in_dim(local_rows[0], lax.axis_index("lat") * band_lats, band_lats)
     answered = fourier_work(lat_rows, my_rows, cosines, sines, wavenumbers, truncation)
     answered = answered.reshape(groups, pair_count, band_lats, 2, channels)

time: 804 us -> 831 us (1.034)
  local copies, waits for them, and re-layouts: 68.9 us -> 98.4 us
    another operation x0 -> x9, local copies, waits for them, and re-layouts: none -> 22.7 us  [local(): jnp.stack(jnp.split(fourier, lax.axis_size('lat'), axis=1))]
where the time goes in v1:
time: 831 us; the launch traced here: 825 us
  matrix products  459 us (55%)
  waiting for transfers between devices  220 us (26%)
  local copies, waits for them, and re-layouts  98.4 us (12%)
  other arithmetic  22 us (3%)
  between operations  14.2 us (2%)
  starting transfers between devices  10.6 us (1%)
    dot_general x1, matrix products, fourier_work(): jnp.einsum('lfk,psk->plsf', products, sines, preferred_element_type=jnp.f...  108 us
    dot_general x1, matrix products, fourier_work(): jnp.einsum('plsf,psk->lfk', imag_part, sines, preferred_element_type=jnp....  104 us
    dot_general x1, matrix products, fourier_work(): jnp.einsum('plsf,psk->lfk', real_part, cosines, preferred_element_type=jn...  103 us
    dot_general x1, matrix products, fourier_work(): jnp.einsum('lfk,psk->plsf', products, cosines, preferred_element_type=jnp...  103 us
    reduce_scatter x1, waiting for transfers between devices, local(): lax.psum_scatter(jnp.moveaxis(picked_tiles, 0, 1).reshape(local_channels...  92.7 us
    all_gather x1, waiting for transfers between devices, local(): gathered = lax.all_gather(spec_in, 'lev', axis=0, tiled=True)  57.7 us
    while x20, matrix products  41.2 us
    all_to_all x1, waiting for transfers between devices, local(): lax.all_to_all(answered, 'lat', split_axis=0, concat_axis=0, tiled=True)  34.7 us
  transfers between devices with their start and end apart: 4, of which 4 were waited for; matrix products, arithmetic and copies ran while one was open for 0% of the time, Pallas kernels for 0%

profile of v1, /device:TPU:2, one launch (start us, length us, event | category | flops | bytes accessed | tf_op | source)
XLA Modules:
  0.0 825.4 jit_solution(10463734065259561108)
XLA Ops:
  7.7 2.7 fusion.74
  10.4 57.7 %all-gather.2.cloned.1.call-done = bf16[32,80,1281]{2,1,0:T(8,128)(2,1)} async-done(((bf16[1,80,1281]{2,1,0:T(8,128)(2,1)}), bf16[32,80,1281]{2,1,0:T(8,128)(2,1)}) %all-gather.2.cloned.1.call-update) | async-done | bytes 6558736 | tf_op jit(solution)/shard_map/all_gather | solution.py:79
  68.2 7.4 copy.54
  75.6 45.1 %while.20 = (s32[]{:T(128)}, f32[10,8,40,4,32]{2,4,3,1,0:T(8,128)}, bf16[10,8,40,1281]{3,2,1,0:T(8,128)(2,1)}, bf16[10,32,8,1281]{3,1,2,0:T(8,128)(2,1)}, bf16[10,8,1281,4]{2,3,1,0:T(4,128)(2,1)S(1)}, /*index=5*/s32[]{:T(128)}) while((s32[]{:T(128)}, f32[10,8,40,4,32]{2,4,3,1,0:T(8,128)}, bf16[10,8,40,1281]{3,2,1,0:T(8,128)(2,1)}, ...), condition=%wide.region_1.2_spmd, body=%wide.region_0.1_spmd.sunk | while | flops 106251264 | bytes 9575181 | solution.py:90
  120.7 3.3 subtract_convert_fusion
  124.0 3.1 slice_bitcast_fusion.3
  127.1 2.9 copy.35
  130.7 2.9 copy.36
  133.6 2.9 copy.37
  138.1 3.1 fusion.76
  141.2 3.7 copy.39
  144.8 3.4 copy.40
  157.1 7.0 all-to-all-start
  164.6 34.4 %all-to-all-done = bf16[8,80,10,2,32]{1,4,3,2,0:T(8,128)(2,1)S(1)} async-done(((bf16[8,80,10,2,32]{1,4,3,2,0:T(8,128)(2,1)}), bf16[8,80,10,2,32]{1,4,3,2,0:T(8,128)(2,1)S(1)}, u32[]{:S(2)}, u32[]{:S(2)}) %all-to-all-start) | async-done | bytes 819232 | tf_op jit(solution)/shard_map/all_to_all | solution.py:101
  201.1 103.7 %fusion.27 = f32[10,16,5120]{2,1,0:T(8,128)S(1)} fusion(s32[640,2]{0,1:T(2,128)S(1)} %get-tuple-element.98, bf16[640,10,2,16]{0,3,2,1:T(8,128)(2,1)S(1)} %fusion.97), kind=kOutput, calls=%fused_computation.38 | convolution fusion | flops 2162688000 | bytes 3691520 | tf_op jit(solution)/shard_map/plsf,psk->lfk/dot_general | solution.py:45
  304.8 103.3 %fusion.30 = f32[10,16,5120]{2,1,0:T(8,128)S(1)} fusion(f32[10,16,5120]{2,1,0:T(8,128)S(1)} %fusion.27, s32[640,2]{0,1:T(2,128)S(1)} %get-tuple-element.98, bf16[640,10,2,16]{0,3,2,1:T(8,128)(2,1)S(1)} %fusion.99), kind=kOutput, calls=%fused_computation.39 | convolution fusion | flops 2164326400 | bytes 6968320 | tf_op jit(solution)/shard_map/plsf,psk->lfk/dot_general | solution.py:40
  410.0 103.2 %fusion.41 = f32[640,10,2,16]{0,3,1,2:T(8,128)S(1)} fusion(s32[640,2]{0,1:T(2,128)S(1)} %get-tuple-element.98, bf16[10,16,5120,1]{2,1,0,3:T(8,128)(2,1)S(1)} %maximum_bitcast_fusion.9), kind=kOutput, calls=%fused_computation.63 | convolution fusion | flops 2162892800 | bytes 2462720 | tf_op jit(solution)/shard_map/lfk,psk->plsf/dot_general | solution.py:54
  514.0 107.7 %fusion.50 = f32[640,10,2,16]{0,3,1,2:T(8,128)S(1)} fusion(s32[640,2]{0,1:T(2,128)S(1)} %get-tuple-element.98, bf16[10,16,5120,1]{2,1,0,3:T(8,128)(2,1)} %maximum_bitcast_fusion.10), kind=kOutput, calls=%fused_computation.66 | convolution fusion | flops 2163097600 | bytes 2462720 | tf_op jit(solution)/shard_map/lfk,psk->plsf/dot_general | solution.py:58
  624.2 3.6 all-to-all-start.1
  627.8 34.7 %all-to-all-done.1 = bf16[8,80,10,2,32]{1,4,3,2,0:T(8,128)(2,1)S(1)} async-done(((bf16[8,80,10,2,32]{1,4,3,2,0:T(8,128)(2,1)}), bf16[8,80,10,2,32]{1,4,3,2,0:T(8,128)(2,1)S(1)}, u32[]{:S(2)}, u32[]{:S(2)}) %all-to-all-start.1) | async-done | bytes 819232 | tf_op jit(solution)/shard_map/all_to_all | solution.py:107
  664.4 6.0 copy.45
  670.4 46.5 %while.21 = (s32[]{:T(128)}, bf16[10,32,8,1281]{3,1,2,0:T(8,128)(2,1)}, bf16[10,8,40,1281]{3,2,1,0:T(8,128)(2,1)}, bf16[10,8,40,4,32]{2,4,3,1,0:T(8,128)(2,1)S(1)}, f32[10,8,1281,4]{2,3,1,0:T(4,128)}, /*index=5*/s32[]{:T(128)}) while((s32[]{:T(128)}, bf16[10,32,8,1281]{3,1,2,0:T(8,128)(2,1)}, bf16[10,8,40,1281]{3,2,1,0:T(8,128)(2,1)}, ...), condition=%wide.region_4.5_spmd, body=%wide.region_2.4_spmd.sunk | while | flops 107235072 | bytes 14686669 | solution.py:128
  716.8 8.4 %copy.53 = bf16[32,10,8,1281]{3,2,1,0:T(8,128)(2,1)} copy(bf16[32,10,8,1281]{3,0,2,1:T(8,128)(2,1)} %bitcast.123) | data formatting | bytes 13117440 | tf_op jit(solution)/shard_map/convert_element_type | solution.py:132
  725.3 92.7 %reduce-scatter.2.cloned.1.call-done = bf16[1,80,1281]{2,1,0:T(8,128)(2,1)} async-done(((bf16[32,80,1281]{2,1,0:T(8,128)(2,1)}), bf16[1,80,1281]{2,1,0:T(8,128)(2,1)}) %reduce-scatter.2.cloned.1.call-update) | async-done | bytes 204976 | tf_op jit(solution)/shard_map/reduce_scatter | solution.py:129
  (150 shorter events, 112.7 us)
Async XLA Ops:
  6.5 61.6 %all-gather.2.cloned.1.call-start = ((), (), s32[]{:S(2)}) async-start(), calls=%async_computation.3 | async-start | bytes 7434240 | tf_op jit(solution)/shard_map/all_gather | solution.py:79
  141.2 7.0 copy-start
  149.8 14.3 %copy-start.2 = (s32[2,40]{1,0:T(2,128)S(1)}, s32[2,40]{1,0:T(2,128)}, u32[]{:S(2)}) copy-start(s32[2,40]{1,0:T(2,128)} %param.13) | copy-start | bytes 964
  157.1 41.8 %all-to-all-start = ((bf16[8,80,10,2,32]{1,4,3,2,0:T(8,128)(2,1)}), bf16[8,80,10,2,32]{1,4,3,2,0:T(8,128)(2,1)S(1)}, u32[]{:S(2)}, u32[]{:S(2)}) async-start(bf16[8,80,10,2,32]{1,4,3,2,0:T(8,128)(2,1)} %bitcast_dynamic-update-slice_fusion.1), calls=%async_computation | async-start | bytes 2621440 | tf_op jit(solution)/shard_map/all_to_all | solution.py:101
  622.6 39.9 %copy-start.1 = (f32[40]{0:T(128)S(1)}, f32[40]{0:T(128)}, u32[]{:S(2)}) copy-start(f32[40]{0:T(128)} %param.12) | copy-start | bytes 484
  624.2 38.3 %all-to-all-start.1 = ((bf16[8,80,10,2,32]{1,4,3,2,0:T(8,128)(2,1)}), bf16[8,80,10,2,32]{1,4,3,2,0:T(8,128)(2,1)S(1)}, u32[]{:S(2)}, u32[]{:S(2)}) async-start(bf16[8,80,10,2,32]{1,4,3,2,0:T(8,128)(2,1)} %fusion.33), calls=%async_computation.1 | async-start | bytes 2621440 | tf_op jit(solution)/shard_map/all_to_all | solution.py:107
  627.8 190.2 %reduce-scatter.2.cloned.1.call-start = ((), (), s32[]{:S(2)}) async-start(), calls=%async_computation.4 | async-start | bytes 7434240 | tf_op jit(solution)/shard_map/reduce_scatter | solution.py:129
Sparse Core Ops, SparseCore 0:
  10.0 58.1 all-gather.1
  725.4 92.5 reduce-scatter.1
